TPU v7x, 32 devices: a whole 2x2x4 slice. The times are simulated.
32 devices in a mesh: dom: 8 (over z, core), cls: 4 (over y, x).
Axes of the slice: x: 2, y: 2, z: 4, core: 2. Of those that a mesh axis runs over, the one named last changes fastest.
Arguments:
- particles: bfloat16 [8192, 9216], P('dom'), may hold values from -6 to 6
- defocus: float32 [8192], P('dom'), may hold values from 0.5 to 2
- inv_noise: float32 [4608], replicated, may hold values from 0.25 to 4
- references: bfloat16 [96, 8, 9216], P(('cls', 'dom')), may hold values from -0.125 to 0.125
- part_class: int32 [8192], P('dom'), may hold values from 0 to 95, as said below
- part_rot: int32 [8192], P('dom'), may hold values from 0 to 7
- counts: int32 [96], replicated, may hold values from 0 to 399
Outputs:
- best_score: float32 [8192], P('dom')
- class_images: float32 [96, 8, 9216], P(('cls', 'dom'))
Inputs may be any that keep to these rules, and one draw needn't show every extreme that they name: `part_class`: block o of classes is o * 3 to o * 3 + 2. In each aligned block of 1024 particles at most 96 have their class in any one block of classes; in every draw one block of classes receives exactly 96 from every block of particles.
All inputs are finite; a program needn't handle non-finite values.
Results may differ from a plain program's by a relative error of at most 0.0044.
Values may be sent and summed in bfloat16 or wider, within the bound.
No kernel may reach another device: no remote copies, remote signals or barrier semaphores. Data moves between devices by JAX's collectives and lax.ppermute only.
A program may use at most 192 MiB of HBM per device.

v0:
```python
import jax
import jax.numpy as jnp
from jax import lax
from jax.sharding import PartitionSpec as P


def frequencies(pixels):
    positions = jnp.arange(pixels, dtype=jnp.int32)
    row_offset = (positions // 64 - pixels // 128).astype(jnp.float32)
    column = (positions % 64).astype(jnp.float32)
    return (row_offset * row_offset + column * column) / 4096.0


def contrast(defocus, inv_noise):
    phase_shift = 12.0 * defocus[:, None] * frequencies(inv_noise.shape[0])[None, :]
    return -0.995 * jnp.sin(phase_shift) - 0.1 * jnp.cos(phase_shift)


def power_spectrum(images, pixels):
    real_part = images[..., :pixels].astype(jnp.float32)
    imag_part = images[..., pixels:].astype(jnp.float32)
    return (real_part * real_part + imag_part * imag_part).astype(jnp.bfloat16)


def on_device(particles, defocus, inv_noise, references, part_class, part_rot, counts):
    local_rows = particles.shape[0]
    pixels = inv_noise.shape[0]
    owned = references.shape[0]
    rotations = references.shape[1]
    dom_size = lax.axis_size("dom")
    cls_size = lax.axis_size("cls")
    cls_index = lax.axis_index("cls")
    contrast_rows = contrast(defocus, inv_noise)
    factor = inv_noise[None, :] * contrast_rows
    weighted = (particles.astype(jnp.float32) * jnp.concatenate([factor, factor], axis=1)).astype(
        jnp.bfloat16
    )
    power_weight = (factor * contrast_rows).astype(jnp.bfloat16)
    class_total = counts.shape[0]
    log_prior = jnp.log(
        (counts + 1).astype(jnp.float32) / (jnp.sum(counts) + class_total).astype(jnp.float32)
    )
    block_first = cls_index * (dom_size * owned)
    images = lax.all_gather(references, "dom", axis=0, tiled=True)
    power = power_spectrum(images, pixels)
    held = images.shape[0]
    flat_images = images.reshape(held * rotations, 2 * pixels)
    flat_power = power.reshape(held * rotations, pixels)
    cross_term = lax.dot_general(
        flat_images, weighted, (((1,), (1,)), ((), ())), preferred_element_type=jnp.float32
    )
    power_term = lax.dot_general(
        flat_power, power_weight, (((1,), (1,)), ((), ())), preferred_element_type=jnp.float32
    )
    class_prior = lax.dynamic_slice_in_dim(log_prior, block_first, held)
    score = cross_term - 0.5 * power_term + jnp.repeat(class_prior, rotations)[:, None]
    local_best = jnp.max(score, axis=0)
    best_score = lax.pmax(local_best, "cls")
    capacity = max(2, 3 * local_rows // (dom_size * cls_size))
    owner_ids = part_class // owned
    target = owner_ids % dom_size
    is_mine = owner_ids // dom_size == cls_index
    pose_code = part_class % owned * rotations + part_rot + 1
    dest_hits = (
        (target[:, None] == jnp.arange(dom_size, dtype=jnp.int32)[None, :]) & is_mine[:, None]
    ).astype(jnp.int32)
    earlier = jnp.cumsum(dest_hits, axis=0) - dest_hits
    rank_within = jnp.sum(earlier * dest_hits, axis=1)
    slot_count = dom_size * capacity
    slot_of = jnp.where(is_mine, target * capacity + rank_within, slot_count)
    source_row = (
        jnp.full((slot_count + 1,), local_rows, jnp.int32)
        .at[slot_of]
        .set(jnp.arange(local_rows, dtype=jnp.int32))[:slot_count]
    )
    filled = source_row < local_rows
    safe_row = jnp.minimum(source_row, local_rows - 1)
    empty_value = jnp.zeros((), jnp.bfloat16)
    send_weighted = jnp.where(filled[:, None], jnp.take(weighted, safe_row, axis=0), empty_value)
    send_code = jnp.where(filled, jnp.take(pose_code, safe_row), 0).astype(jnp.bfloat16)
    pose_ids = jnp.arange(owned * rotations, dtype=jnp.int32) + 1
    send_power = jnp.where(filled[:, None], jnp.take(power_weight, safe_row, axis=0), empty_value)
    payload = jnp.concatenate([send_weighted, send_power], axis=1).reshape(
        dom_size, capacity, 3 * pixels
    )
    arrived, arrived_code = (
        lax.all_to_all(payload, "dom", split_axis=0, concat_axis=0, tiled=True),
        lax.all_to_all(
            send_code.reshape(dom_size, capacity), "dom", split_axis=0, concat_axis=0, tiled=True
        ),
    )
    arrived = arrived.reshape(slot_count, 3 * pixels)
    codes = arrived_code.reshape(slot_count).astype(jnp.int32)
    selector = (pose_ids[:, None] == codes[None, :]).astype(jnp.bfloat16)
    sums = jnp.dot(selector, arrived, preferred_element_type=jnp.float32)
    numerator = sums[:, : 2 * pixels]
    denominator = sums[:, 2 * pixels :]
    images = numerator / (jnp.concatenate([denominator, denominator], axis=1) + 1.0)
    return (best_score, images.reshape(owned, rotations, 2 * pixels))


def solution(mesh):
    placed = (P("dom", None), P("dom"), P(), P(("cls", "dom"), None, None), P("dom"), P("dom"), P())
    return jax.shard_map(
        on_device,
        mesh=mesh,
        in_specs=placed,
        out_specs=(P("dom"), P(("cls", "dom"), None, None)),
        check_vma=False,
    )
```

profile of v0, /device:TPU:0, one launch (start us, length us, event | category | flops | bytes accessed | tf_op | source)
XLA Modules:
  0.0 712.4 jit_solution(14085966261514725436)
XLA Ops:
  7.2 0.7 fusion.68
  7.9 0.7 fusion.55
  8.6 0.7 fusion.58
  9.3 2.3 reduce-window.6
  12.2 0.7 compare_select_fusion.3
  12.9 4.3 scatter_custom_fusion
  17.3 3.2 gather_fusion
  21.3 6.3 all-to-all-start
  28.5 72.0 %fusion.6 = (bf16[1024,4608]{1,0:T(8,128)(2,1)}, f32[1024,4608]{1,0:T(8,128)}) fusion(f32[4608]{0:T(1024)S(1)} %fusion.51, f32[1024]{0:T(1024)S(1)} %broadcast_multiply_fusion, f32[4608]{0:T(1024)} %param.9), kind=kLoop, calls=%fused_computation.14 | loop fusion | flops 33030144 | bytes 28352512 | tf_op jit(solution)/shard_map/convert_element_type | solution.py:38
  100.5 18.4 %gather_fusion.2 = bf16[768,4608]{1,0:T(8,128)(2,1)} fusion(bf16[1024,4608]{1,0:T(8,128)(2,1)} %get-tuple-element.2, s32[1024]{0:T(1024)S(1)} %pad_clamp_fusion), kind=kCustom, calls=%fused_computation.2 | custom fusion | bytes 14158848 | tf_op jit(solution)/shard_map/jit(_take)/gather | solution.py:82
  118.8 25.8 %fusion = bf16[1024,9216]{1,0:T(8,128)(2,1)} fusion(f32[1024,4608]{1,0:T(8,128)} %get-tuple-element.3, bf16[1024,9216]{1,0:T(8,128)(2,1)} %param.7), kind=kLoop, calls=%fused_computation.5 | loop fusion | flops 37748736 | bytes 56623104 | tf_op jit(solution)/shard_map/convert_element_type | solution.py:35
  144.6 33.5 %gather_fusion.1 = bf16[768,9216]{1,0:T(8,128)(2,1)} fusion(bf16[1024,9216]{1,0:T(8,128)(2,1)} %fusion, s32[1024]{0:T(1024)S(1)} %pad_clamp_fusion), kind=kCustom, calls=%fused_computation.1 | custom fusion | bytes 28314624 | tf_op jit(solution)/shard_map/jit(_take)/gather | solution.py:79
  178.1 3.9 select_select_fusion.1
  182.0 7.1 select_select_fusion
  189.1 12.6 %pad_maximum_fusion = bf16[8,96,13824]{2,1,0:T(8,128)(2,1)} fusion(bf16[8,96,4608]{2,1,0:T(8,128)(2,1)S(1)} %select_select_fusion.1, bf16[8,96,9216]{2,1,0:T(8,128)(2,1)S(1)} %select_select_fusion), kind=kLoop, calls=%fused_computation.8 | loop fusion | flops 42467328 | bytes 42467328 | tf_op jit(solution)/shard_map/concatenate | solution.py:83
  201.8 6.3 all-to-all-start.1
  210.4 72.9 %all-gather.2.cloned.1.call-done = bf16[24,8,9216]{2,1,0:T(8,128)(2,1)} async-done(((bf16[3,8,9216]{2,1,0:T(8,128)(2,1)}), bf16[24,8,9216]{2,1,0:T(8,128)(2,1)}) %all-gather.2.cloned.1.call-update) | async-done | bytes 3538960 | tf_op jit(solution)/shard_map/all_gather | solution.py:44
  283.3 2.8 fusion.75
  286.2 71.7 %fusion.14 = f32[192,1024]{1,0:T(8,128)S(1)} fusion(f32[4608]{0:T(1024)S(1)} %fusion.51, f32[1024]{0:T(1024)S(1)} %broadcast_multiply_fusion, f32[4608]{0:T(1024)S(1)} %copy-done.1, bf16[192,4608]{1,0:T(8,128)(2,1)S(1)} %fusion.75), kind=kOutput, calls=%fused_computation.24 | convolution fusion | flops 1845166080 | bytes 2596864 | tf_op jit(solution)/shard_map/dot_general | solution.py:52
  357.9 6.3 fusion.26
  364.2 10.4 %pmax.7 = f32[1024]{0:T(1024)} all-reduce(f32[1024]{0:T(1024)S(1)} %fusion.26), channel_id=1, replica_groups=mesh['dom'=8,'cls'=4] {'cls'}, use_global_device_ids=true, to_apply=%region_2.3 | all-reduce | flops 1024 | bytes 8192 | tf_op jit(solution)/shard_map/pmax | solution.py:58
  374.7 320.9 %all-to-all-done.1 = bf16[8,96,13824]{2,1,0:T(8,128)(2,1)} async-done(((bf16[8,96,13824]{2,1,0:T(8,128)(2,1)}), bf16[8,96,13824]{2,1,0:T(8,128)(2,1)}, u32[]{:S(2)}, u32[]{:S(2)}) %all-to-all-start.1) | async-done | bytes 21233696 | tf_op jit(solution)/shard_map/all_to_all | solution.py:87
  695.6 8.6 %fusion.31 = f32[24,13824]{1,0:T(8,128)S(1)} fusion(bf16[768,13824]{1,0:T(8,128)(2,1)} %bitcast.8, s32[768]{0:T(1024)S(1)} %reshape.180, s32[24]{0:T(128)S(1)} %iota_add_fusion), kind=kOutput, calls=%fused_computation.32 | convolution fusion | flops 509626368 | bytes 22563936 | tf_op jit(solution)/shard_map/dot_general | solution.py:95
  704.3 1.1 fusion.29
  (48 shorter events, 4.1 us)
Async XLA Ops:
  21.3 180.5 %all-to-all-start = ((bf16[8,1,96]{2,1,0:T(2,128)(2,1)}), bf16[8,1,96]{2,1,0:T(2,128)(2,1)S(1)}, u32[]{:S(2)}, u32[]{:S(2)}) async-start(bf16[8,1,96]{2,1,0:T(2,128)(2,1)} %copy.9), calls=%async_computation | async-start | bytes 8192 | tf_op jit(solution)/shard_map/all_to_all | solution.py:88
  201.8 7.0 copy-start.2
  201.8 84.3 %copy-start.1 = (f32[4608]{0:T(1024)S(1)}, f32[4608]{0:T(1024)}, u32[]{:S(2)}) copy-start(f32[4608]{0:T(1024)} %param.9) | copy-start | bytes 55300
  201.8 493.9 %all-to-all-start.1 = ((bf16[8,96,13824]{2,1,0:T(8,128)(2,1)}), bf16[8,96,13824]{2,1,0:T(8,128)(2,1)}, u32[]{:S(2)}, u32[]{:S(2)}) async-start(bf16[8,96,13824]{2,1,0:T(8,128)(2,1)} %pad_maximum_fusion), calls=%async_computation.1 | async-start | bytes 42467328 | tf_op jit(solution)/shard_map/all_to_all | solution.py:87
  208.0 75.3 %all-gather.2.cloned.1.call-start = ((), (), s32[]{:S(2)}) async-start(), calls=%async_computation.2 | async-start | bytes 3981312 | tf_op jit(solution)/shard_map/all_gather | solution.py:44
  283.3 74.6 %slice-start = ((s8[18874368]{0:T(1024)(128)(4,1)}), s8[4194304]{0:T(1024)(128)(4,1)S(1)}, s32[]{:S(2)}) async-start(s8[18874368]{0:T(1024)(128)(4,1)} %bitcast.59), calls=%async_computation.3 | async-start | bytes 8388608
  286.1 71.8 %slice-start.1 = ((s8[18874368]{0:T(1024)(128)(4,1)}), s8[4194304]{0:T(1024)(128)(4,1)S(1)}, s32[]{:S(2)}) async-start(s8[18874368]{0:T(1024)(128)(4,1)} %bitcast.59), calls=%async_computation.4 | async-start | bytes 8388608
  286.1 71.8 %slice-start.2 = ((s8[18874368]{0:T(1024)(128)(4,1)}), s8[4194304]{0:T(1024)(128)(4,1)S(1)}, s32[]{:S(2)}) async-start(s8[18874368]{0:T(1024)(128)(4,1)} %bitcast.59), calls=%async_computation.5 | async-start | bytes 8388608
  286.1 71.8 %slice-start.3 = ((s8[18874368]{0:T(1024)(128)(4,1)}), s8[4194304]{0:T(1024)(128)(4,1)S(1)}, s32[]{:S(2)}) async-start(s8[18874368]{0:T(1024)(128)(4,1)} %bitcast.59), calls=%async_computation.6 | async-start | bytes 8388608
  286.1 71.8 %slice-start.4 = ((s8[18874368]{0:T(1024)(128)(4,1)}), s8[2097152]{0:T(1024)(128)(4,1)S(1)}, s32[]{:S(2)}) async-start(s8[18874368]{0:T(1024)(128)(4,1)} %bitcast.59), calls=%async_computation.7 | async-start | bytes 4194304
  286.1 71.8 %copy-start = (bf16[24,8,9216]{2,1,0:T(8,128)(2,1)S(1)}, bf16[24,8,9216]{2,1,0:T(8,128)(2,1)}, u32[]{:S(2)}) copy-start(bf16[24,8,9216]{2,1,0:T(8,128)(2,1)} %all-gather.2.cloned.1.call-done) | copy-start | bytes 10616836
Sparse Core Ops, SparseCore 0:
  210.5 72.7 all-gather.1
where the time goes:
time: 722 us; the launch traced here: 712 us
  waiting for transfers between devices  394 us (55%)
  other arithmetic  132 us (18%)
  matrix products  86.6 us (12%)
  local copies, waits for them, and re-layouts  61 us (8%)
  between operations  15.2 us (2%)
  starting transfers between devices  12.6 us (2%)
  blocking collectives  10.4 us (1%)
    all_to_all x1, waiting for transfers between devices, on_device(): lax.all_to_all(payload, 'dom', split_axis=0, concat_axis=0, tiled=True)  321 us
    all_gather x1, waiting for transfers between devices, on_device(): images = lax.all_gather(references, 'dom', axis=0, tiled=True)  72.9 us
    convert_element_type x1, other arithmetic, on_device(): power_weight = (factor * contrast_rows).astype(jnp.bfloat16)  72 us
    dot_general x1, matrix products, on_device(): lax.dot_general(flat_power, power_weight, (((1,), (1,)), ((), ())), prefe...  71.7 us
    gather x1, local copies, waits for them, and re-layouts, on_device(): jnp.take(weighted, safe_row, axis=0)  33.5 us
    convert_element_type x1, other arithmetic, on_device(): (particles.astype(jnp.float32) * jnp.concatenate([factor, factor], axis=1...  25.8 us
    gather x1, local copies, waits for them, and re-layouts, on_device(): jnp.take(power_weight, safe_row, axis=0)  18.4 us
  transfers between devices with their start and end apart: 3, of which 2 were waited for; matrix products, arithmetic and copies ran while one was open for 36% of the time, Pallas kernels for 0%

commit v1 on v0

--- a/solution.py
+++ b/solution.py
@@ -41,7 +41,9 @@
         (counts + 1).astype(jnp.float32) / (jnp.sum(counts) + class_total).astype(jnp.float32)
     )
     block_first = cls_index * (dom_size * owned)
-    images = lax.all_gather(references, "dom", axis=0, tiled=True)
+    images = jnp.concatenate(
+        lax.all_to_all(jnp.stack(lax.axis_size("dom") * [references]), "dom", 0, 0), axis=0
+    )
     power = power_spectrum(images, pixels)
     held = images.shape[0]
     flat_images = images.reshape(held * rotations, 2 * pixels)

time: 722 us -> 744 us (1.030)
  waiting for transfers between devices: 394 us -> 422 us
  between operations: 15.2 us -> 1.79 us
    all_gather x1 -> x0, waiting for transfers between devices: 72.9 us -> none  [on_device(): images = lax.all_gather(references, 'dom', axis=0, tiled=True)]
    all_to_all x0 -> x1, waiting for transfers between devices: none -> 56.5 us  [on_device(): lax.all_to_all(jnp.stack(lax.axis_size('dom') * [references]), 'dom', 0, 0)]
    all_to_all x1, waiting for transfers between devices: 321 us -> 366 us  [on_device(): lax.all_to_all(payload, 'dom', split_axis=0, concat_axis=0, tiled=True)]
  transfers between devices with their start and end apart: 3 -> 3, of which waited for: 2 -> 2; matrix products, arithmetic and copies ran while one was open for 36% -> 35% of each run, Pallas kernels for 0% -> 0%
where the time goes in v1:
time: 744 us; the launch traced here: 734 us
  waiting for transfers between devices  422 us (57%)
  other arithmetic  130 us (17%)
  matrix products  87.8 us (12%)
  local copies, waits for them, and re-layouts  64.2 us (9%)
  starting transfers between devices  17.7 us (2%)
  blocking collectives  10.5 us (1%)
    all_to_all x1, waiting for transfers between devices, on_device(): lax.all_to_all(payload, 'dom', split_axis=0, concat_axis=0, tiled=True)  366 us
    dot_general x1, matrix products, on_device(): lax.dot_general(flat_power, power_weight, (((1,), (1,)), ((), ())), prefe...  72.9 us
    convert_element_type x1, other arithmetic, on_device(): power_weight = (factor * contrast_rows).astype(jnp.bfloat16)  72 us
    all_to_all x1, waiting for transfers between devices, on_device(): lax.all_to_all(jnp.stack(lax.axis_size('dom') * [references]), 'dom', 0, 0)  56.5 us
    gather x1, local copies, waits for them, and re-layouts, on_device(): jnp.take(weighted, safe_row, axis=0)  33.5 us
    convert_element_type x1, other arithmetic, on_device(): (particles.astype(jnp.float32) * jnp.concatenate([factor, factor], axis=1...  25.4 us
    gather x1, local copies, waits for them, and re-layouts, on_device(): jnp.take(power_weight, safe_row, axis=0)  18.8 us
  transfers between devices with their start and end apart: 3, of which 2 were waited for; matrix products, arithmetic and copies ran while one was open for 35% of the time, Pallas kernels for 0%

profile of v1, /device:TPU:0, one launch (start us, length us, event | category | flops | bytes accessed | tf_op | source)
XLA Modules:
  0.0 734.3 jit_solution(10821687753335570573)
XLA Ops:
  1.3 0.7 fusion.44
  2.1 0.7 fusion.47
  2.8 2.3 reduce-window.6
  5.6 0.7 compare_select_fusion.3
  6.3 4.3 scatter_custom_fusion
  10.8 3.2 gather_fusion
  14.7 6.3 all-to-all-start.1
  21.9 72.0 %fusion.6 = (bf16[1024,4608]{1,0:T(8,128)(2,1)}, f32[1024,4608]{1,0:T(8,128)}) fusion(f32[4608]{0:T(1024)S(1)} %fusion.40, f32[1024]{0:T(1024)S(1)} %broadcast_multiply_fusion, f32[4608]{0:T(1024)} %param.9), kind=kLoop, calls=%fused_computation.14 | loop fusion | flops 33030144 | bytes 28352512 | tf_op jit(solution)/shard_map/convert_element_type | solution.py:38
  93.8 25.4 %fusion = bf16[1024,9216]{1,0:T(8,128)(2,1)} fusion(f32[1024,4608]{1,0:T(8,128)} %get-tuple-element.3, bf16[1024,9216]{1,0:T(8,128)(2,1)} %param.7), kind=kLoop, calls=%fused_computation.5 | loop fusion | flops 37748736 | bytes 56623104 | tf_op jit(solution)/shard_map/convert_element_type | solution.py:35
  119.3 18.8 %gather_fusion.2 = bf16[768,4608]{1,0:T(8,128)(2,1)} fusion(bf16[1024,4608]{1,0:T(8,128)(2,1)} %get-tuple-element.2, s32[1024]{0:T(1024)S(1)} %pad_clamp_fusion), kind=kCustom, calls=%fused_computation.2 | custom fusion | bytes 14158848 | tf_op jit(solution)/shard_map/jit(_take)/gather | solution.py:84
  138.1 33.5 %gather_fusion.1 = bf16[768,9216]{1,0:T(8,128)(2,1)} fusion(bf16[1024,9216]{1,0:T(8,128)(2,1)} %fusion, s32[1024]{0:T(1024)S(1)} %pad_clamp_fusion), kind=kCustom, calls=%fused_computation.1 | custom fusion | bytes 28314624 | tf_op jit(solution)/shard_map/jit(_take)/gather | solution.py:81
  171.7 2.1 stack.2
  173.8 5.3 all-to-all-start
  179.1 3.9 select_select_fusion.1
  183.1 7.1 select_select_fusion
  190.1 12.4 %pad_maximum_fusion = bf16[8,96,13824]{2,1,0:T(8,128)(2,1)} fusion(bf16[8,96,4608]{2,1,0:T(8,128)(2,1)S(1)} %select_select_fusion.1, bf16[8,96,9216]{2,1,0:T(8,128)(2,1)S(1)} %select_select_fusion), kind=kLoop, calls=%fused_computation.8 | loop fusion | flops 42467328 | bytes 42467328 | tf_op jit(solution)/shard_map/concatenate | solution.py:85
  202.6 56.5 %all-to-all-done = bf16[8,3,8,9216]{3,2,1,0:T(8,128)(2,1)S(1)} async-done(((bf16[8,3,8,9216]{3,2,1,0:T(8,128)(2,1)}), bf16[8,3,8,9216]{3,2,1,0:T(8,128)(2,1)S(1)}, u32[]{:S(2)}, u32[]{:S(2)}) %all-to-all-start) | async-done | bytes 3538976 | tf_op jit(solution)/shard_map/all_to_all | solution.py:45
  259.0 6.1 all-to-all-start.2
  268.8 72.9 %fusion.12 = f32[192,1024]{1,0:T(8,128)S(1)} fusion(f32[4608]{0:T(1024)} %copy-done.1, f32[1024]{0:T(1024)S(1)} %broadcast_multiply_fusion, f32[4608]{0:T(1024)} %param.9, bf16[192,4608]{1,0:T(8,128)(2,1)S(1)} %fusion.65), kind=kOutput, calls=%fused_computation.22 | convolution fusion | flops 1845166080 | bytes 2596864 | tf_op jit(solution)/shard_map/dot_general | solution.py:54
  341.7 6.3 fusion.17
  348.1 10.5 %pmax.7 = f32[1024]{0:T(1024)} all-reduce(f32[1024]{0:T(1024)S(1)} %fusion.17), channel_id=1, replica_groups=mesh['dom'=8,'cls'=4] {'cls'}, use_global_device_ids=true, to_apply=%region_2.3 | all-reduce | flops 1024 | bytes 8192 | tf_op jit(solution)/shard_map/pmax | solution.py:60
  358.6 365.8 %all-to-all-done.2 = bf16[8,96,13824]{2,1,0:T(8,128)(2,1)} async-done(((bf16[8,96,13824]{2,1,0:T(8,128)(2,1)}), bf16[8,96,13824]{2,1,0:T(8,128)(2,1)}, u32[]{:S(2)}, u32[]{:S(2)}) %all-to-all-start.2) | async-done | bytes 21233696 | tf_op jit(solution)/shard_map/all_to_all | solution.py:89
  724.3 8.6 %fusion.20 = f32[24,13824]{1,0:T(8,128)S(1)} fusion(bf16[768,13824]{1,0:T(8,128)(2,1)} %bitcast.9, s32[768]{0:T(1024)S(1)} %reshape.182, s32[24]{0:T(128)S(1)} %iota_add_fusion), kind=kOutput, calls=%fused_computation.30 | convolution fusion | flops 509626368 | bytes 22563936 | tf_op jit(solution)/shard_map/dot_general | solution.py:97
  733.0 1.1 fusion.18
  (52 shorter events, 6.0 us)
Async XLA Ops:
  14.7 156.9 %all-to-all-start.1 = ((bf16[8,1,96]{2,1,0:T(2,128)(2,1)}), bf16[8,1,96]{2,1,0:T(2,128)(2,1)S(1)}, u32[]{:S(2)}, u32[]{:S(2)}) async-start(bf16[8,1,96]{2,1,0:T(2,128)(2,1)} %copy.9), calls=%async_computation.1 | async-start | bytes 8192 | tf_op jit(solution)/shard_map/all_to_all | solution.py:90
  21.1 98.1 %copy-start.1 = (f32[4608]{0:T(1024)}, f32[4608]{0:T(1024)S(1)}, u32[]{:S(2)}) copy-start(f32[4608]{0:T(1024)S(1)} %fusion.40) | copy-start | bytes 55300
  138.1 33.5 %copy-start = (bf16[3,8,9216]{2,1,0:T(8,128)(2,1)S(1)}, bf16[3,8,9216]{2,1,0:T(8,128)(2,1)}, u32[]{:S(2)}) copy-start(bf16[3,8,9216]{2,1,0:T(8,128)(2,1)} %param.10) | copy-start | bytes 1327108
  171.7 2.2 copy-start.2
  173.8 85.2 %all-to-all-start = ((bf16[8,3,8,9216]{3,2,1,0:T(8,128)(2,1)}), bf16[8,3,8,9216]{3,2,1,0:T(8,128)(2,1)S(1)}, u32[]{:S(2)}, u32[]{:S(2)}) async-start(bf16[8,3,8,9216]{3,2,1,0:T(8,128)(2,1)} %stack.2), calls=%async_computation | async-start | bytes 7077888 | tf_op jit(solution)/shard_map/all_to_all | solution.py:45
  202.6 62.6 %copy-start.4 = (s32[96]{0:T(128)S(1)}, s32[96]{0:T(128)}, u32[]{:S(2)}) copy-start(s32[96]{0:T(128)} %param.13) | copy-start | bytes 1156
  259.0 465.3 %all-to-all-start.2 = ((bf16[8,96,13824]{2,1,0:T(8,128)(2,1)}), bf16[8,96,13824]{2,1,0:T(8,128)(2,1)}, u32[]{:S(2)}, u32[]{:S(2)}) async-start(bf16[8,96,13824]{2,1,0:T(8,128)(2,1)} %pad_maximum_fusion), calls=%async_computation.2 | async-start | bytes 42467328 | tf_op jit(solution)/shard_map/all_to_all | solution.py:89
  268.1 73.6 %slice-start = ((s8[18874368]{0:T(1024)(128)(4,1)}), s8[4194304]{0:T(1024)(128)(4,1)S(1)}, s32[]{:S(2)}) async-start(s8[18874368]{0:T(1024)(128)(4,1)} %bitcast.51), calls=%async_computation.3 | async-start | bytes 8388608
  268.7 72.9 %slice-start.1 = ((s8[18874368]{0:T(1024)(128)(4,1)}), s8[4194304]{0:T(1024)(128)(4,1)S(1)}, s32[]{:S(2)}) async-start(s8[18874368]{0:T(1024)(128)(4,1)} %bitcast.51), calls=%async_computation.4 | async-start | bytes 8388608
  268.8 72.9 %slice-start.2 = ((s8[18874368]{0:T(1024)(128)(4,1)}), s8[4194304]{0:T(1024)(128)(4,1)S(1)}, s32[]{:S(2)}) async-start(s8[18874368]{0:T(1024)(128)(4,1)} %bitcast.51), calls=%async_computation.5 | async-start | bytes 8388608
  268.8 72.9 %slice-start.3 = ((s8[18874368]{0:T(1024)(128)(4,1)}), s8[4194304]{0:T(1024)(128)(4,1)S(1)}, s32[]{:S(2)}) async-start(s8[18874368]{0:T(1024)(128)(4,1)} %bitcast.51), calls=%async_computation.6 | async-start | bytes 8388608
  268.8 72.9 %slice-start.4 = ((s8[18874368]{0:T(1024)(128)(4,1)}), s8[2097152]{0:T(1024)(128)(4,1)S(1)}, s32[]{:S(2)}) async-start(s8[18874368]{0:T(1024)(128)(4,1)} %bitcast.51), calls=%async_computation.7 | async-start | bytes 4194304
  268.8 72.9 %copy-start.3 = (f32[192]{0:T(256)S(1)}, f32[192]{0:T(256)}, u32[]{:S(2)}) copy-start(f32[192]{0:T(256)} %add.125) | copy-start | bytes 2308
